TPU v7x, 32 devices: a whole 2x2x4 slice. The times are simulated.
32 devices in a mesh: blk: 16 (over z, y, core), rep: 2 (over x).
Axes of the slice: x: 2, y: 2, z: 4, core: 2. Of those that a mesh axis runs over, the one named last changes fastest.
Arguments:
- qm_pos: float32 [3, 2048], P(None, 'blk'), may hold values from -4 to 4
- species: int32 [2048], P('blk'), may hold values from 0 to 7
- qm_count: int32 [16], P('blk'), may hold values from 64 to 128, as said below
- ghost_owner: int32 [2048, 4], P('blk'), may hold values from 0 to 15, all different within a row; in each aligned block of 128 rows (0 to 127, 128 to 255, ...) at most 64 rows name the same one
- ghost_slot: int32 [2048, 4], P('blk'), may hold values from 0 to 127
- mm_pos: float32 [3, 16384], P(None, ('blk', 'rep')), may hold values from -4 to 4
- mm_charge: float32 [16384], P(('blk', 'rep')), may hold values from -6 to 6
- species_table: bfloat16 [8, 128], replicated, may hold values from -6 to 6
- potential_gain: float32 [128], replicated, may hold values from -8 to 8
- message_weight: bfloat16 [128, 128], replicated, may hold values from -0.25 to 0.25
- hidden_weight: bfloat16 [128, 256], replicated, may hold values from -0.5 to 0.5
- energy_readout: float32 [256], replicated, may hold values from -0.375 to 0.375
- charge_readout: float32 [256], replicated, may hold values from -0.375 to 0.375
Outputs:
- atom_energy: float32 [2048], P('blk')
- qm_force: float32 [3, 2048], P(None, 'blk')
- mm_force: float32 [3, 16384], P(None, ('blk', 'rep'))
Inputs may be any that keep to these rules, and one draw needn't show every extreme that they name: `qm_count`: some block holds exactly 128 live atoms. `ghost_owner`: each row names 4 different blocks; among the rows of one device no block is named more than 64 times, and some block exactly 64 times.
All inputs are finite; a program needn't handle non-finite values.
Results may differ from a plain program's by a relative error of at most 0.0055.
Values may be sent and summed in bfloat16 or wider, within the bound.
No kernel may reach another device: no remote copies, remote signals or barrier semaphores. Data moves between devices by JAX's collectives and lax.ppermute only.
A program may use at most 64 MiB of HBM per device.

v0:
```python
import math
import jax
import jax.numpy as jnp
from jax import lax
from jax.sharding import PartitionSpec as P

SOFTEN = 0.25


def pair_parts(qm_places, mm_places):
    offset = qm_places[:, :, None] - mm_places[:, None, :]
    inverse = lax.rsqrt(jnp.sum(offset * offset, axis=0) + SOFTEN)
    return (offset, inverse)


def split_columns(stacked, limit):
    stride = math.gcd(stacked.shape[1], limit)
    shaped = stacked.reshape(stacked.shape[0], stacked.shape[1] // stride, stride)
    return jnp.transpose(shaped, (1, 0, 2))


def potential_from(qm_places, mm_stack):

    def potential_advance(running, columns):
        offset, inverse = pair_parts(qm_places, columns[:3])
        return (running + jnp.sum(inverse * columns[3][None, :], axis=1), None)

    result, _ = lax.scan(
        potential_advance,
        jnp.zeros((qm_places.shape[1],), jnp.float32),
        split_columns(mm_stack, 512),
    )
    return result


def on_device(
    qm_pos,
    species,
    qm_count,
    ghost_owner,
    ghost_slot,
    mm_pos,
    mm_charge,
    species_table,
    potential_gain,
    message_weight,
    hidden_weight,
    energy_readout,
    charge_readout,
):
    atom_rows = qm_pos.shape[1]
    blocks = lax.axis_size("blk")
    neighbours = ghost_owner.shape[1]
    channels = species_table.shape[1]
    capacity = 2 * atom_rows * neighbours // blocks
    coupling = float(mm_pos.shape[1] * blocks * lax.axis_size("rep")) ** (-0.5)
    mm_stack = jnp.concatenate([mm_pos, mm_charge[None, :]], axis=0)
    partial_sum = potential_from(qm_pos, lax.all_gather(mm_stack, "blk", axis=1, tiled=True))
    potential = lax.psum(partial_sum, "rep") * coupling
    live = (jnp.arange(atom_rows) < qm_count[0]).astype(jnp.float32)
    picks = (species[:, None] == jnp.arange(species_table.shape[0])[None, :]).astype(jnp.bfloat16)
    base = jnp.dot(picks, species_table, preferred_element_type=jnp.float32)
    start = (live[:, None] * (base + potential[:, None] * potential_gain[None, :])).astype(
        jnp.bfloat16
    )
    owners = ghost_owner.reshape(-1)
    slots = ghost_slot.reshape(-1)
    hits = (owners[:, None] == jnp.arange(blocks)[None, :]).astype(jnp.int32)
    ranks = jnp.sum((jnp.cumsum(hits, axis=0) - hits) * hits, axis=1)
    request = jnp.zeros((blocks, capacity), jnp.int32).at[owners, ranks].set(slots)
    wanted = lax.all_to_all(request, "blk", split_axis=0, concat_axis=0, tiled=True)
    outgoing = jnp.take(start, wanted, axis=0)
    arrived = lax.all_to_all(outgoing, "blk", split_axis=0, concat_axis=0, tiled=True)
    ghosts = arrived[owners, ranks]
    neighbour = jnp.sum(
        ghosts.reshape(atom_rows, neighbours, channels).astype(jnp.float32), axis=1
    ).astype(jnp.bfloat16)
    mixed = start.astype(jnp.float32) + jnp.dot(
        neighbour, message_weight, preferred_element_type=jnp.float32
    )
    before = jnp.dot(mixed.astype(jnp.bfloat16), hidden_weight, preferred_element_type=jnp.float32)
    sigma = jax.nn.sigmoid(before)
    active = before * sigma
    energy_part = live * jnp.sum(active * energy_readout[None, :], axis=1)
    charge_part = live * jnp.sum(active * charge_readout[None, :], axis=1)
    atom_energy = energy_part + charge_part * potential
    back_active = live[:, None] * (
        energy_readout[None, :] + potential[:, None] * charge_readout[None, :]
    )
    back_before = (back_active * sigma * (1.0 + before * (1.0 - sigma))).astype(jnp.bfloat16)
    back_mixed = jnp.dot(back_before, hidden_weight.T, preferred_element_type=jnp.float32)
    back_sum = jnp.dot(
        back_mixed.astype(jnp.bfloat16), message_weight.T, preferred_element_type=jnp.float32
    ).astype(jnp.bfloat16)
    outgoing_grads = (
        jnp.zeros((blocks, capacity, channels), jnp.bfloat16)
        .at[owners, ranks]
        .set(jnp.repeat(back_sum, neighbours, axis=0))
    )
    returned = lax.all_to_all(outgoing_grads, "blk", split_axis=0, concat_axis=0, tiled=True)
    picks_back = (wanted.reshape(-1)[:, None] == jnp.arange(atom_rows)[None, :]).astype(
        jnp.bfloat16
    )
    collected = jnp.einsum(
        "ra,rf->af",
        picks_back,
        returned.reshape(blocks * capacity, channels),
        preferred_element_type=jnp.float32,
    )
    back_start = back_mixed + collected
    effective = charge_part + live * jnp.sum(back_start * potential_gain[None, :], axis=1)
    qm_stack = jnp.concatenate([qm_pos, effective[None, :]], axis=0)
    portion = lax.all_gather(qm_stack, "blk", axis=1, tiled=True)
    mm_running = jnp.zeros((3, mm_pos.shape[1]), jnp.float32)

    def add_advance(running, group):
        offset, inverse = pair_parts(group[:3], mm_pos)
        weight = inverse * inverse * inverse * mm_charge[None, :]
        pull = jnp.sum(offset * weight[None], axis=2) * group[3][None, :]
        running = running - jnp.sum(offset * (weight * group[3][:, None])[None], axis=1)
        return (running, pull)

    mm_running, pulls = lax.scan(add_advance, mm_running, split_columns(portion, 512))
    block_terms = jnp.transpose(pulls, (1, 0, 2)).reshape(3, portion.shape[1])
    qm_terms = block_terms
    mm_sum, qm_terms = (mm_running, qm_terms)
    block_force = lax.psum_scatter(qm_terms, "blk", scatter_dimension=1, tiled=True)
    qm_force = lax.psum(block_force, "rep") * coupling
    return (atom_energy, qm_force, mm_sum * coupling)


def solution(mesh):
    placed = (
        P(None, "blk"),
        P("blk"),
        P("blk"),
        P("blk", None),
        P("blk", None),
        P(None, ("blk", "rep")),
        P(("blk", "rep")),
        P(),
        P(),
        P(),
        P(),
        P(),
        P(),
    )
    return jax.shard_map(
        on_device,
        mesh=mesh,
        in_specs=placed,
        out_specs=(P("blk"), P(None, "blk"), P(None, ("blk", "rep"))),
        check_vma=False,
    )
```

profile of v0, /device:TPU:0, one launch (start us, length us, event | category | flops | bytes accessed | tf_op | source)
XLA Modules:
  0.0 304.6 jit_solution(3147633748383444944)
XLA Ops:
  7.2 0.8 copy.36
  8.3 1.2 reduce-window.6
  9.8 0.8 copy.40
  11.4 69.8 %scatter_fusion = s32[16,64]{1,0:T(8,128)} fusion(s32[16,64]{1,0:T(8,128)} %broadcast_in_dim.31, s32[512]{0:T(512)S(1)} %bitcast.80, s32[512]{0:T(512)S(1)} %reshape.281), kind=kCustom, calls=%fused_computation.2 | custom fusion | bytes 10240 | tf_op jit(solution)/shard_map/scatter | solution.py:70
  81.2 7.4 %all-to-all-start = ((s32[16,1,64]{2,1,0:T(1,128)}), s32[16,1,64]{2,1,0:T(1,128)S(1)}, u32[]{:S(2)}, u32[]{:S(2)}) async-start(s32[16,1,64]{2,1,0:T(1,128)} %bitcast.8), calls=%async_computation | async-start | bytes 16384 | tf_op jit(solution)/shard_map/all_to_all | solution.py:71
  88.6 22.1 %all_gather.6 = f32[4,8192]{1,0:T(4,128)S(1)} all-gather(f32[4,512]{1,0:T(4,128)S(1)} %pad_maximum_fusion), channel_id=1, replica_groups=mesh['blk'=16,'rep'=2] {'blk'}, dimensions={1}, use_global_device_ids=true | all-gather | bytes 139264 | tf_op jit(solution)/shard_map/all_gather | solution.py:58
  110.7 5.4 %while.24 = (s32[]{:T(128)}, f32[128]{0:T(128)S(1)}, f32[3,128]{1,0:T(4,128)S(1)}, f32[16,4,512]{2,1,0:T(4,128)S(1)}, s32[]{:T(128)}, /*index=5*/s32[]{:T(128)}, s32[]{}) while((s32[]{:T(128)}, f32[128]{0:T(128)S(1)}, f32[3,128]{1,0:T(4,128)S(1)}, f32[16,4,512]{2,1,0:T(4,128)S(1)}, s32[]{:T(128)}, /*index=5*/s32[]{:T(128)}, ...), condition=%wide.region_3.4_spmd.clone, body=%wide.region_0.3_spmd.clone.sunk | while | flops 721028 | bytes 552567 | solution.py:28
  116.1 4.9 %psum.14 = f32[128]{0:T(128)S(1)} all-reduce(f32[128]{0:T(128)S(1)} %get-tuple-element.58), channel_id=1, replica_groups=mesh['blk'=16,'rep'=2] {'rep'}, use_global_device_ids=true, to_apply=%region_4.5 | all-reduce | flops 128 | bytes 1024 | tf_op jit(solution)/shard_map/psum | solution.py:59
  122.1 3.2 %gather_fusion = bf16[1024,128]{1,0:T(8,128)(2,1)S(1)} fusion(bf16[128,128]{1,0:T(8,128)(2,1)S(1)} %fusion.8, s32[1024]{0:T(1024)S(1)} %broadcast_clamp_fusion), kind=kCustom, calls=%fused_computation | custom fusion | bytes 528384 | tf_op jit(solution)/shard_map/jit(_take)/gather | solution.py:72
  125.5 12.8 %all_to_all.25 = bf16[16,64,128]{2,1,0:T(8,128)(2,1)S(1)} all-to-all(bf16[16,64,128]{2,1,0:T(8,128)(2,1)S(1)} %broadcast_select_fusion.1), channel_id=1, replica_groups=mesh['blk'=16,'rep'=2] {'blk'}, dimensions={0} | all-to-all | bytes 524288 | tf_op jit(solution)/shard_map/all_to_all | solution.py:73
  138.3 3.2 %gather_fusion.1 = bf16[512,128]{1,0:T(8,128)(2,1)S(1)} fusion(bf16[16,64,128]{2,1,0:T(8,128)(2,1)S(1)} %all_to_all.25, s32[512]{0:T(512)S(1)} %bitcast.82), kind=kCustom, calls=%fused_computation.1 | custom fusion | bytes 266240 | tf_op jit(solution)/shard_map/gather | solution.py:74
  143.3 52.6 %scatter_fusion.1 = bf16[16,64,128]{2,1,0:T(8,128)(2,1)} fusion(bf16[16,64,128]{2,1,0:T(8,128)(2,1)} %broadcast_in_dim.37, s32[512]{0:T(512)S(1)} %bitcast.81, bf16[512,128]{1,0:T(8,128)(2,1)S(1)} %bitcast.85), kind=kCustom, calls=%fused_computation.3 | custom fusion | bytes 397312 | tf_op jit(solution)/shard_map/scatter | solution.py:98
  195.9 3.5 %all-to-all-start.2 = ((bf16[16,64,128]{2,1,0:T(8,128)(2,1)}), bf16[16,64,128]{2,1,0:T(8,128)(2,1)S(1)}, u32[]{:S(2)}, u32[]{:S(2)}) async-start(bf16[16,64,128]{2,1,0:T(8,128)(2,1)} %scatter_fusion.1), calls=%async_computation.2 | async-start | bytes 524288 | tf_op jit(solution)/shard_map/all_to_all | solution.py:100
  201.3 8.1 %all-to-all-done.2 = bf16[16,64,128]{2,1,0:T(8,128)(2,1)S(1)} async-done(((bf16[16,64,128]{2,1,0:T(8,128)(2,1)}), bf16[16,64,128]{2,1,0:T(8,128)(2,1)S(1)}, u32[]{:S(2)}, u32[]{:S(2)}) %all-to-all-start.2) | async-done | bytes 262176 | tf_op jit(solution)/shard_map/all_to_all | solution.py:100
  210.0 18.8 %all_gather.7 = f32[4,2048]{1,0:T(4,128)S(1)} all-gather(f32[4,128]{1,0:T(4,128)S(1)} %pad_maximum_fusion.1), channel_id=1, replica_groups=mesh['blk'=16,'rep'=2] {'blk'}, dimensions={1}, use_global_device_ids=true | all-gather | bytes 34816 | tf_op jit(solution)/shard_map/all_gather | solution.py:113
  228.8 6.3 %while.25 = (s32[]{:T(128)}, f32[3,512]{1,0:T(4,128)S(1)}, f32[4,3,512]{2,1,0:T(4,128)S(1)}, f32[4,4,512]{2,1,0:T(4,128)S(1)}, f32[3,512]{1,0:T(4,128)S(1)}, /*index=5*/f32[512]{0:T(512)S(1)}, s32[]{:T(128)}, s32[]{:T(128)}, s32[]{}) while((s32[]{:T(128)}, f32[3,512]{1,0:T(4,128)S(1)}, f32[4,3,512]{2,1,0:T(4,128)S(1)}, ...), condition=%wide.region_18.19_spmd.clone, body=%wide.region_14.18_spmd.clone.sunk | while | flops 7341572 | bytes 6385803 | solution.py:123
  229.4 0.9 fusion.40
  231.0 0.9 fusion.40
  232.5 0.9 fusion.40
  234.1 0.9 fusion.40
  235.1 1.4 copy.46
  237.1 54.2 %reduce-scatter.4.cloned.1.call-done = f32[128,3]{1,0:T(8,128)} async-done(((f32[2048,3]{1,0:T(8,128)}), f32[128,3]{1,0:T(8,128)}) %reduce-scatter.4.cloned.1.call-update) | async-done | bytes 1552
  291.3 0.9 copy.47
  292.2 4.9 %psum.15 = f32[3,128]{1,0:T(4,128)S(1)} all-reduce(f32[3,128]{1,0:T(4,128)S(1)} %copy.47), channel_id=1, replica_groups=mesh['blk'=16,'rep'=2] {'rep'}, use_global_device_ids=true, to_apply=%region_20.21 | all-reduce | flops 384 | bytes 3072 | tf_op jit(solution)/shard_map/psum | solution.py:128
  (166 shorter events, 14.7 us)
Async XLA Ops:
  7.2 134.5 %copy-start = (bf16[128,256]{1,0:T(8,128)(2,1)S(1)}, bf16[128,256]{1,0:T(8,128)(2,1)}, u32[]{:S(2)}) copy-start(bf16[128,256]{1,0:T(8,128)(2,1)} %param.27) | copy-start | bytes 196612
  11.4 77.2 %copy-start.1 = (f32[3,512]{1,0:T(4,128)S(1)}, f32[3,512]{1,0:T(4,128)}, u32[]{:S(2)}) copy-start(f32[3,512]{1,0:T(4,128)} %param.22) | copy-start | bytes 18436
  11.4 77.2 %copy-start.3 = (f32[512]{0:T(512)S(1)}, f32[512]{0:T(512)}, u32[]{:S(2)}) copy-start(f32[512]{0:T(512)} %param.23) | copy-start | bytes 6148
  11.4 99.3 %copy-start.2 = (f32[3,128]{1,0:T(4,128)S(1)}, f32[3,128]{1,0:T(4,128)}, u32[]{:S(2)}) copy-start(f32[3,128]{1,0:T(4,128)} %param.17) | copy-start | bytes 4612
  81.2 40.8 %all-to-all-start = ((s32[16,1,64]{2,1,0:T(1,128)}), s32[16,1,64]{2,1,0:T(1,128)S(1)}, u32[]{:S(2)}, u32[]{:S(2)}) async-start(s32[16,1,64]{2,1,0:T(1,128)} %bitcast.8), calls=%async_computation | async-start | bytes 16384 | tf_op jit(solution)/shard_map/all_to_all | solution.py:71
  110.7 11.0 %copy-start.5 = (bf16[8,128]{1,0:T(8,128)(2,1)S(1)}, bf16[8,128]{1,0:T(8,128)(2,1)}, u32[]{:S(2)}) copy-start(bf16[8,128]{1,0:T(8,128)(2,1)} %param.24) | copy-start | bytes 6148
  110.7 11.0 %copy-start.8 = (s32[128]{0:T(128)S(1)}, s32[128]{0:T(128)}, u32[]{:S(2)}) copy-start(s32[128]{0:T(128)} %param.18) | copy-start | bytes 1540
  110.7 11.0 %copy-start.9 = (f32[128]{0:T(128)S(1)}, f32[128]{0:T(128)}, u32[]{:S(2)}) copy-start(f32[128]{0:T(128)} %param.25) | copy-start | bytes 1540
  125.5 16.2 %copy-start.4 = (bf16[128,128]{1,0:T(8,128)(2,1)S(1)}, bf16[128,128]{1,0:T(8,128)(2,1)}, u32[]{:S(2)}) copy-start(bf16[128,128]{1,0:T(8,128)(2,1)} %param.26) | copy-start | bytes 98308
  125.5 16.2 %copy-start.6 = (f32[256]{0:T(256)S(1)}, f32[256]{0:T(256)}, u32[]{:S(2)}) copy-start(f32[256]{0:T(256)} %param.28) | copy-start | bytes 3076
  125.5 16.2 %copy-start.7 = (f32[256]{0:T(256)S(1)}, f32[256]{0:T(256)}, u32[]{:S(2)}) copy-start(f32[256]{0:T(256)} %param.29) | copy-start | bytes 3076
  195.9 13.5 %all-to-all-start.2 = ((bf16[16,64,128]{2,1,0:T(8,128)(2,1)}), bf16[16,64,128]{2,1,0:T(8,128)(2,1)S(1)}, u32[]{:S(2)}, u32[]{:S(2)}) async-start(bf16[16,64,128]{2,1,0:T(8,128)(2,1)} %scatter_fusion.1), calls=%async_computation.2 | async-start | bytes 524288 | tf_op jit(solution)/shard_map/all_to_all | solution.py:100
  199.4 91.9 %reduce-scatter.4.cloned.1.call-start = ((), (), s32[]{:S(2)}) async-start(), calls=%async_computation.4 | async-start | bytes 1114112
Sparse Core Ops, SparseCore 0:
  236.6 54.6 reduce-scatter.3
where the time goes:
time: 307 us; the launch traced here: 305 us
  local copies, waits for them, and re-layouts  136 us (44%)
  blocking collectives  63.5 us (21%)
  waiting for transfers between devices  62.3 us (20%)
  between operations  15 us (5%)
  other arithmetic  14.6 us (5%)
  starting transfers between devices  11 us (4%)
    scatter x1, local copies, waits for them, and re-layouts, on_device(): jnp.zeros((blocks, capacity), jnp.int32).at[owners, ranks].set(slots)  69.8 us
    unnamed x2, waiting for transfers between devices  54.3 us
    scatter x1, local copies, waits for them, and re-layouts, on_device(): outgoing_grads = jnp.zeros((blocks, capacity, channels), jnp.bfloat16).at...  52.6 us
    all_gather x1, blocking collectives, on_device(): lax.all_gather(mm_stack, 'blk', axis=1, tiled=True)  22.1 us
    all_gather x1, blocking collectives, on_device(): portion = lax.all_gather(qm_stack, 'blk', axis=1, tiled=True)  18.8 us
    all_to_all x1, blocking collectives, on_device(): lax.all_to_all(outgoing, 'blk', split_axis=0, concat_axis=0, tiled=True)  12.8 us
    all_to_all x1, waiting for transfers between devices, on_device(): lax.all_to_all(outgoing_grads, 'blk', split_axis=0, concat_axis=0, tiled=...  8.06 us
    all_to_all x1, starting transfers between devices, on_device(): lax.all_to_all(request, 'blk', split_axis=0, concat_axis=0, tiled=True)  7.38 us
  transfers between devices with their start and end apart: 3, of which 2 were waited for; matrix products, arithmetic and copies ran while one was open for 2% of the time, Pallas kernels for 0%

commit v1 on v0

--- a/solution.py
+++ b/solution.py
@@ -68,7 +68,19 @@
     hits = (owners[:, None] == jnp.arange(blocks)[None, :]).astype(jnp.int32)
     ranks = jnp.sum((jnp.cumsum(hits, axis=0) - hits) * hits, axis=1)
     request = jnp.zeros((blocks, capacity), jnp.int32).at[owners, ranks].set(slots)
-    wanted = lax.all_to_all(request, "blk", split_axis=0, concat_axis=0, tiled=True)
+    ways, here = (lax.axis_size("blk"), lax.axis_index("blk"))
+    width = request.shape[0] // ways
+    dims = list(request.shape)
+    dims[0] = width
+    height = dims[0]
+    dims[0] = height * ways
+    full = jnp.zeros(dims, request.dtype)
+    for mask in range(ways):
+        part = lax.dynamic_slice_in_dim(request, (here ^ mask) * width, width, axis=0)
+        if mask:
+            part = lax.ppermute(part, "blk", [(d, d ^ mask) for d in range(ways)])
+        full = lax.dynamic_update_slice_in_dim(full, part, (here ^ mask) * height, axis=0)
+    wanted = full
     outgoing = jnp.take(start, wanted, axis=0)
     arrived = lax.all_to_all(outgoing, "blk", split_axis=0, concat_axis=0, tiled=True)
     ghosts = arrived[owners, ranks]

time: 307 us -> 281 us (0.915)
  local copies, waits for them, and re-layouts: 136 us -> 90.8 us
  starting transfers between devices: 11 us -> 24.7 us
  waiting for transfers between devices: 62.3 us -> 66.3 us
    scatter x1, local copies, waits for them, and re-layouts: 69.8 us -> 25.3 us  [on_device(): jnp.zeros((blocks, capacity), jnp.int32).at[owners, ranks].set(slots)]
    ppermute x0 -> x15, starting transfers between devices: none -> 21.1 us  [on_device(): part = lax.ppermute(part, 'blk', [(d, d ^ mask) for d in range(ways)])]
    all_to_all x1 -> x0, starting transfers between devices: 7.38 us -> none  [on_device(): lax.all_to_all(request, 'blk', split_axis=0, concat_axis=0, tiled=True)]
  transfers between devices with their start and end apart: 3 -> 17, of which waited for: 2 -> 3; matrix products, arithmetic and copies ran while one was open for 2% -> 2% of each run, Pallas kernels for 0% -> 0%
where the time goes in v1:
time: 281 us; the launch traced here: 280 us
  local copies, waits for them, and re-layouts  90.8 us (32%)
  blocking collectives  66.3 us (24%)
  waiting for transfers between devices  66.3 us (24%)
  starting transfers between devices  24.7 us (9%)
  between operations  15.2 us (5%)
  other arithmetic  14 us (5%)
    unnamed x2, waiting for transfers between devices  54.3 us
    scatter x1, local copies, waits for them, and re-layouts, on_device(): outgoing_grads = jnp.zeros((blocks, capacity, channels), jnp.bfloat16).at...  52.6 us
    scatter x1, local copies, waits for them, and re-layouts, on_device(): jnp.zeros((blocks, capacity), jnp.int32).at[owners, ranks].set(slots)  25.3 us
    all_gather x1, blocking collectives, on_device(): lax.all_gather(mm_stack, 'blk', axis=1, tiled=True)  22.1 us
    ppermute x15, starting transfers between devices, on_device(): part = lax.ppermute(part, 'blk', [(d, d ^ mask) for d in range(ways)])  21.1 us
    all_gather x1, blocking collectives, on_device(): portion = lax.all_gather(qm_stack, 'blk', axis=1, tiled=True)  18.8 us
    all_to_all x1, blocking collectives, on_device(): lax.all_to_all(outgoing, 'blk', split_axis=0, concat_axis=0, tiled=True)  15.5 us
    all_to_all x1, waiting for transfers between devices, on_device(): lax.all_to_all(outgoing_grads, 'blk', split_axis=0, concat_axis=0, tiled=...  9.25 us
  transfers between devices with their start and end apart: 17, of which 3 were waited for; matrix products, arithmetic and copies ran while one was open for 2% of the time, Pallas kernels for 0%

profile of v1, /device:TPU:0, one launch (start us, length us, event | category | flops | bytes accessed | tf_op | source)
XLA Modules:
  0.0 279.7 jit_solution(16354665460716005134)
XLA Ops:
  8.3 1.2 reduce-window.6
  11.0 25.3 %scatter_fusion = s32[16,64]{1,0:T(8,128)S(1)} fusion(s32[16,64]{1,0:T(8,128)S(1)} %broadcast.158.clone, s32[512]{0:T(512)S(1)} %bitcast.73, s32[512]{0:T(512)S(1)} %reshape.249), kind=kCustom, calls=%fused_computation.2 | custom fusion | bytes 10240 | tf_op jit(solution)/shard_map/scatter | solution.py:70
  36.9 2.6 collective-permute-start.1
  39.6 1.8 collective-permute-start.3
  41.4 22.1 %all_gather.6 = f32[4,8192]{1,0:T(4,128)S(1)} all-gather(f32[4,512]{1,0:T(4,128)S(1)} %pad_maximum_fusion), channel_id=1, replica_groups=mesh['blk'=16,'rep'=2] {'blk'}, dimensions={1}, use_global_device_ids=true | all-gather | bytes 139264 | tf_op jit(solution)/shard_map/all_gather | solution.py:58
  63.5 5.4 %while.24 = (s32[]{:T(128)}, f32[128]{0:T(128)S(1)}, f32[3,128]{1,0:T(4,128)S(1)}, f32[16,4,512]{2,1,0:T(4,128)S(1)}, s32[]{:T(128)}, /*index=5*/s32[]{:T(128)}, s32[]{}) while((s32[]{:T(128)}, f32[128]{0:T(128)S(1)}, f32[3,128]{1,0:T(4,128)S(1)}, f32[16,4,512]{2,1,0:T(4,128)S(1)}, s32[]{:T(128)}, /*index=5*/s32[]{:T(128)}, ...), condition=%wide.region_3.4_spmd.clone, body=%wide.region_0.3_spmd.clone.sunk | while | flops 721028 | bytes 552567 | solution.py:28
  68.9 4.9 %psum.14 = f32[128]{0:T(128)S(1)} all-reduce(f32[128]{0:T(128)S(1)} %get-tuple-element.58), channel_id=1, replica_groups=mesh['blk'=16,'rep'=2] {'rep'}, use_global_device_ids=true, to_apply=%region_4.5 | all-reduce | flops 128 | bytes 1024 | tf_op jit(solution)/shard_map/psum | solution.py:59
  74.9 1.5 collective-permute-start.6
  76.5 3.9 %collective-permute-start.8 = (s32[1,64]{1,0:T(1,128)S(1)}, s32[1,64]{1,0:T(1,128)S(1)}, u32[]{:S(2)}, u32[]{:S(2)}) collective-permute-start(s32[1,64]{1,0:T(1,128)S(1)} %get-tuple-element.131), channel_id=1, source_target_pairs={{0,18},{2,16},{4,22},{6,20},{8,26},{10,24},{12,30},{14,28},{16,2},... | collective-permute-start | bytes 776 | tf_op jit(solution)/shard_map/ppermute | solution.py:81
  80.6 2.4 collective-permute-start.10
  83.4 4.4 %collective-permute-start.12 = (s32[1,64]{1,0:T(1,128)S(1)}, s32[1,64]{1,0:T(1,128)S(1)}, u32[]{:S(2)}, u32[]{:S(2)}) collective-permute-start(s32[1,64]{1,0:T(1,128)S(1)} %get-tuple-element.127), channel_id=1, source_target_pairs={{0,26},{2,24},{4,30},{6,28},{8,18},{10,16},{12,22},{14,20},{16,10}... | collective-permute-start | bytes 776 | tf_op jit(solution)/shard_map/ppermute | solution.py:81
  88.1 3.2 %collective-permute-start.14 = (s32[1,64]{1,0:T(1,128)S(1)}, s32[1,64]{1,0:T(1,128)S(1)}, u32[]{:S(2)}, u32[]{:S(2)}) collective-permute-start(s32[1,64]{1,0:T(1,128)S(1)} %get-tuple-element.125), channel_id=1, source_target_pairs={{0,30},{2,28},{4,26},{6,24},{8,22},{10,20},{12,18},{14,16},{16,14}... | collective-permute-start | bytes 776 | tf_op jit(solution)/shard_map/ppermute | solution.py:81
  91.4 2.7 collective-permute-done.13
  94.3 3.2 %gather_fusion = bf16[1024,128]{1,0:T(8,128)(2,1)S(1)} fusion(bf16[128,128]{1,0:T(8,128)(2,1)S(1)} %fusion.8, s32[1024]{0:T(1024)S(1)} %broadcast_clamp_fusion), kind=kCustom, calls=%fused_computation | custom fusion | bytes 528384 | tf_op jit(solution)/shard_map/jit(_take)/gather | solution.py:84
  97.8 15.5 %all_to_all.10 = bf16[16,64,128]{2,1,0:T(8,128)(2,1)S(1)} all-to-all(bf16[16,64,128]{2,1,0:T(8,128)(2,1)S(1)} %broadcast_select_fusion.1), channel_id=1, replica_groups=mesh['blk'=16,'rep'=2] {'blk'}, dimensions={0} | all-to-all | bytes 524288 | tf_op jit(solution)/shard_map/all_to_all | solution.py:85
  113.4 3.2 %gather_fusion.1 = bf16[512,128]{1,0:T(8,128)(2,1)S(1)} fusion(bf16[16,64,128]{2,1,0:T(8,128)(2,1)S(1)} %all_to_all.10, s32[512]{0:T(512)S(1)} %bitcast.75), kind=kCustom, calls=%fused_computation.1 | custom fusion | bytes 266240 | tf_op jit(solution)/shard_map/gather | solution.py:86
  118.4 52.6 %scatter_fusion.1 = bf16[16,64,128]{2,1,0:T(8,128)(2,1)} fusion(bf16[16,64,128]{2,1,0:T(8,128)(2,1)} %broadcast_in_dim.34, s32[512]{0:T(512)S(1)} %bitcast.74, bf16[512,128]{1,0:T(8,128)(2,1)S(1)} %bitcast.78), kind=kCustom, calls=%fused_computation.3 | custom fusion | bytes 397312 | tf_op jit(solution)/shard_map/scatter | solution.py:110
  170.9 3.5 %all-to-all-start.1 = ((bf16[16,64,128]{2,1,0:T(8,128)(2,1)}), bf16[16,64,128]{2,1,0:T(8,128)(2,1)S(1)}, u32[]{:S(2)}, u32[]{:S(2)}) async-start(bf16[16,64,128]{2,1,0:T(8,128)(2,1)} %scatter_fusion.1), calls=%async_computation.1 | async-start | bytes 524288 | tf_op jit(solution)/shard_map/all_to_all | solution.py:112
  175.2 9.3 %all-to-all-done.1 = bf16[16,64,128]{2,1,0:T(8,128)(2,1)S(1)} async-done(((bf16[16,64,128]{2,1,0:T(8,128)(2,1)}), bf16[16,64,128]{2,1,0:T(8,128)(2,1)S(1)}, u32[]{:S(2)}, u32[]{:S(2)}) %all-to-all-start.1) | async-done | bytes 262176 | tf_op jit(solution)/shard_map/all_to_all | solution.py:112
  185.1 18.8 %all_gather.7 = f32[4,2048]{1,0:T(4,128)S(1)} all-gather(f32[4,128]{1,0:T(4,128)S(1)} %pad_maximum_fusion.1), channel_id=1, replica_groups=mesh['blk'=16,'rep'=2] {'blk'}, dimensions={1}, use_global_device_ids=true | all-gather | bytes 34816 | tf_op jit(solution)/shard_map/all_gather | solution.py:125
  203.8 6.3 %while.25 = (s32[]{:T(128)}, f32[3,512]{1,0:T(4,128)S(1)}, f32[4,3,512]{2,1,0:T(4,128)S(1)}, f32[4,4,512]{2,1,0:T(4,128)S(1)}, f32[3,512]{1,0:T(4,128)S(1)}, /*index=5*/f32[512]{0:T(512)S(1)}, s32[]{:T(128)}, s32[]{:T(128)}, s32[]{}) while((s32[]{:T(128)}, f32[3,512]{1,0:T(4,128)S(1)}, f32[4,3,512]{2,1,0:T(4,128)S(1)}, ...), condition=%wide.region_18.19_spmd.clone, body=%wide.region_14.18_spmd.clone.sunk | while | flops 7341572 | bytes 6385803 | solution.py:135
  210.2 1.4 copy.44
  212.2 54.2 %reduce-scatter.4.cloned.1.call-done = f32[128,3]{1,0:T(8,128)} async-done(((f32[2048,3]{1,0:T(8,128)}), f32[128,3]{1,0:T(8,128)}) %reduce-scatter.4.cloned.1.call-update) | async-done | bytes 1552
  267.3 4.9 %psum.15 = f32[3,128]{1,0:T(4,128)S(1)} all-reduce(f32[3,128]{1,0:T(4,128)S(1)} %copy.45), channel_id=1, replica_groups=mesh['blk'=16,'rep'=2] {'rep'}, use_global_device_ids=true, to_apply=%region_20.21 | all-reduce | flops 384 | bytes 3072 | tf_op jit(solution)/shard_map/psum | solution.py:140
  (210 shorter events, 21.1 us)
Async XLA Ops:
  7.2 109.5 %copy-start = (bf16[128,256]{1,0:T(8,128)(2,1)S(1)}, bf16[128,256]{1,0:T(8,128)(2,1)}, u32[]{:S(2)}) copy-start(bf16[128,256]{1,0:T(8,128)(2,1)} %param.27) | copy-start | bytes 196612
  10.9 30.4 %copy-start.1 = (f32[3,512]{1,0:T(4,128)S(1)}, f32[3,512]{1,0:T(4,128)}, u32[]{:S(2)}) copy-start(f32[3,512]{1,0:T(4,128)} %param.22) | copy-start | bytes 18436
  11.0 30.4 %copy-start.3 = (f32[512]{0:T(512)S(1)}, f32[512]{0:T(512)}, u32[]{:S(2)}) copy-start(f32[512]{0:T(512)} %param.23) | copy-start | bytes 6148
  11.0 52.5 %copy-start.2 = (f32[3,128]{1,0:T(4,128)S(1)}, f32[3,128]{1,0:T(4,128)}, u32[]{:S(2)}) copy-start(f32[3,128]{1,0:T(4,128)} %param.17) | copy-start | bytes 4612
  36.4 38.4 %collective-permute-start = (s32[1,64]{1,0:T(1,128)S(1)}, s32[1,64]{1,0:T(1,128)S(1)}, u32[]{:S(2)}, u32[]{:S(2)}) collective-permute-start(s32[1,64]{1,0:T(1,128)S(1)} %get-tuple-element.139), channel_id=1, source_target_pairs={{0,2},{2,0},{4,6},{6,4},{8,10},{10,8},{12,14},{14,12},{16,18},{18,... | collective-permute-start | bytes 776 | tf_op jit(solution)/shard_map/ppermute | solution.py:81
  36.9 38.0 %collective-permute-start.1 = (s32[1,64]{1,0:T(1,128)S(1)}, s32[1,64]{1,0:T(1,128)S(1)}, u32[]{:S(2)}, u32[]{:S(2)}) collective-permute-start(s32[1,64]{1,0:T(1,128)S(1)} %get-tuple-element.138), channel_id=1, source_target_pairs={{0,4},{2,6},{4,0},{6,2},{8,12},{10,14},{12,8},{14,10},{16,20},{18,... | collective-permute-start | bytes 776 | tf_op jit(solution)/shard_map/ppermute | solution.py:81
  39.5 36.9 %collective-permute-start.2 = (s32[1,64]{1,0:T(1,128)S(1)}, s32[1,64]{1,0:T(1,128)S(1)}, u32[]{:S(2)}, u32[]{:S(2)}) collective-permute-start(s32[1,64]{1,0:T(1,128)S(1)} %get-tuple-element.137), channel_id=1, source_target_pairs={{0,6},{2,4},{4,2},{6,0},{8,14},{10,12},{12,10},{14,8},{16,22},{18,... | collective-permute-start | bytes 776 | tf_op jit(solution)/shard_map/ppermute | solution.py:81
  39.6 37.0 %collective-permute-start.3 = (s32[1,64]{1,0:T(1,128)S(1)}, s32[1,64]{1,0:T(1,128)S(1)}, u32[]{:S(2)}, u32[]{:S(2)}) collective-permute-start(s32[1,64]{1,0:T(1,128)S(1)} %get-tuple-element.136), channel_id=1, source_target_pairs={{0,8},{2,10},{4,12},{6,14},{8,0},{10,2},{12,4},{14,6},{16,24},{18,... | collective-permute-start | bytes 776 | tf_op jit(solution)/shard_map/ppermute | solution.py:81
  41.4 39.1 %collective-permute-start.4 = (s32[1,64]{1,0:T(1,128)S(1)}, s32[1,64]{1,0:T(1,128)S(1)}, u32[]{:S(2)}, u32[]{:S(2)}) collective-permute-start(s32[1,64]{1,0:T(1,128)S(1)} %get-tuple-element.135), channel_id=1, source_target_pairs={{0,10},{2,8},{4,14},{6,12},{8,2},{10,0},{12,6},{14,4},{16,26},{18,... | collective-permute-start | bytes 776 | tf_op jit(solution)/shard_map/ppermute | solution.py:81
  74.8 5.8 %collective-permute-start.5 = (s32[1,64]{1,0:T(1,128)S(1)}, s32[1,64]{1,0:T(1,128)S(1)}, u32[]{:S(2)}, u32[]{:S(2)}) collective-permute-start(s32[1,64]{1,0:T(1,128)S(1)} %get-tuple-element.134), channel_id=1, source_target_pairs={{0,12},{2,14},{4,8},{6,10},{8,4},{10,6},{12,0},{14,2},{16,28},{18,... | collective-permute-start | bytes 776 | tf_op jit(solution)/shard_map/ppermute | solution.py:81
  74.9 8.1 %collective-permute-start.6 = (s32[1,64]{1,0:T(1,128)S(1)}, s32[1,64]{1,0:T(1,128)S(1)}, u32[]{:S(2)}, u32[]{:S(2)}) collective-permute-start(s32[1,64]{1,0:T(1,128)S(1)} %get-tuple-element.133), channel_id=1, source_target_pairs={{0,14},{2,12},{4,10},{6,8},{8,6},{10,4},{12,2},{14,0},{16,30},{18,... | collective-permute-start | bytes 776 | tf_op jit(solution)/shard_map/ppermute | solution.py:81
  76.4 7.0 %collective-permute-start.7 = (s32[1,64]{1,0:T(1,128)S(1)}, s32[1,64]{1,0:T(1,128)S(1)}, u32[]{:S(2)}, u32[]{:S(2)}) collective-permute-start(s32[1,64]{1,0:T(1,128)S(1)} %get-tuple-element.132), channel_id=1, source_target_pairs={{0,16},{2,18},{4,20},{6,22},{8,24},{10,26},{12,28},{14,30},{16,0},... | collective-permute-start | bytes 776 | tf_op jit(solution)/shard_map/ppermute | solution.py:81
  76.5 11.3 %collective-permute-start.8 = (s32[1,64]{1,0:T(1,128)S(1)}, s32[1,64]{1,0:T(1,128)S(1)}, u32[]{:S(2)}, u32[]{:S(2)}) collective-permute-start(s32[1,64]{1,0:T(1,128)S(1)} %get-tuple-element.131), channel_id=1, source_target_pairs={{0,18},{2,16},{4,22},{6,20},{8,26},{10,24},{12,30},{14,28},{16,2},... | collective-permute-start | bytes 776 | tf_op jit(solution)/shard_map/ppermute | solution.py:81
  80.4 7.6 %collective-permute-start.9 = (s32[1,64]{1,0:T(1,128)S(1)}, s32[1,64]{1,0:T(1,128)S(1)}, u32[]{:S(2)}, u32[]{:S(2)}) collective-permute-start(s32[1,64]{1,0:T(1,128)S(1)} %get-tuple-element.130), channel_id=1, source_target_pairs={{0,20},{2,22},{4,16},{6,18},{8,28},{10,30},{12,24},{14,26},{16,4},... | collective-permute-start | bytes 776 | tf_op jit(solution)/shard_map/ppermute | solution.py:81
  80.6 10.7 %collective-permute-start.10 = (s32[1,64]{1,0:T(1,128)S(1)}, s32[1,64]{1,0:T(1,128)S(1)}, u32[]{:S(2)}, u32[]{:S(2)}) collective-permute-start(s32[1,64]{1,0:T(1,128)S(1)} %get-tuple-element.129), channel_id=1, source_target_pairs={{0,22},{2,20},{4,18},{6,16},{8,30},{10,28},{12,26},{14,24},{16,6},... | collective-permute-start | bytes 776 | tf_op jit(solution)/shard_map/ppermute | solution.py:81
  83.0 8.4 %collective-permute-start.11 = (s32[1,64]{1,0:T(1,128)S(1)}, s32[1,64]{1,0:T(1,128)S(1)}, u32[]{:S(2)}, u32[]{:S(2)}) collective-permute-start(s32[1,64]{1,0:T(1,128)S(1)} %get-tuple-element.128), channel_id=1, source_target_pairs={{0,24},{2,26},{4,28},{6,30},{8,16},{10,18},{12,20},{14,22},{16,8},... | collective-permute-start | bytes 776 | tf_op jit(solution)/shard_map/ppermute | solution.py:81
  83.4 8.0 %collective-permute-start.12 = (s32[1,64]{1,0:T(1,128)S(1)}, s32[1,64]{1,0:T(1,128)S(1)}, u32[]{:S(2)}, u32[]{:S(2)}) collective-permute-start(s32[1,64]{1,0:T(1,128)S(1)} %get-tuple-element.127), channel_id=1, source_target_pairs={{0,26},{2,24},{4,30},{6,28},{8,18},{10,16},{12,22},{14,20},{16,10}... | collective-permute-start | bytes 776 | tf_op jit(solution)/shard_map/ppermute | solution.py:81
  87.9 6.3 %collective-permute-start.13 = (s32[1,64]{1,0:T(1,128)S(1)}, s32[1,64]{1,0:T(1,128)S(1)}, u32[]{:S(2)}, u32[]{:S(2)}) collective-permute-start(s32[1,64]{1,0:T(1,128)S(1)} %get-tuple-element.126), channel_id=1, source_target_pairs={{0,28},{2,30},{4,24},{6,26},{8,20},{10,22},{12,16},{14,18},{16,12}... | collective-permute-start | bytes 776 | tf_op jit(solution)/shard_map/ppermute | solution.py:81
  88.1 6.1 %collective-permute-start.14 = (s32[1,64]{1,0:T(1,128)S(1)}, s32[1,64]{1,0:T(1,128)S(1)}, u32[]{:S(2)}, u32[]{:S(2)}) collective-permute-start(s32[1,64]{1,0:T(1,128)S(1)} %get-tuple-element.125), channel_id=1, source_target_pairs={{0,30},{2,28},{4,26},{6,24},{8,22},{10,20},{12,18},{14,16},{16,14}... | collective-permute-start | bytes 776 | tf_op jit(solution)/shard_map/ppermute | solution.py:81
  97.8 18.9 %copy-start.4 = (bf16[128,128]{1,0:T(8,128)(2,1)S(1)}, bf16[128,128]{1,0:T(8,128)(2,1)}, u32[]{:S(2)}) copy-start(bf16[128,128]{1,0:T(8,128)(2,1)} %param.26) | copy-start | bytes 98308
  97.8 18.9 %copy-start.6 = (f32[256]{0:T(256)S(1)}, f32[256]{0:T(256)}, u32[]{:S(2)}) copy-start(f32[256]{0:T(256)} %param.28) | copy-start | bytes 3076
  97.8 18.9 %copy-start.7 = (f32[256]{0:T(256)S(1)}, f32[256]{0:T(256)}, u32[]{:S(2)}) copy-start(f32[256]{0:T(256)} %param.29) | copy-start | bytes 3076
  170.9 13.5 %all-to-all-start.1 = ((bf16[16,64,128]{2,1,0:T(8,128)(2,1)}), bf16[16,64,128]{2,1,0:T(8,128)(2,1)S(1)}, u32[]{:S(2)}, u32[]{:S(2)}) async-start(bf16[16,64,128]{2,1,0:T(8,128)(2,1)} %scatter_fusion.1), calls=%async_computation.1 | async-start | bytes 524288 | tf_op jit(solution)/shard_map/all_to_all | solution.py:112
  174.5 92.0 %reduce-scatter.4.cloned.1.call-start = ((), (), s32[]{:S(2)}) async-start(), calls=%async_computation.3 | async-start | bytes 1114112
  (3 other events, 33.0 us)
Sparse Core Ops, SparseCore 0:
  211.7 54.6 reduce-scatter.3
